TPU v7x, 256 devices: a whole 4x4x8 slice. The times are simulated.
256 devices in a mesh: row: 16 (over x, z_hi, core), col: 4 (over y), rep: 4 (over z_lo).
Axes of the slice: x: 4, y: 4, z: 8 (z_hi: 2, z_lo: 4; z = z_hi * 4 + z_lo), core: 2. Of those that a mesh axis runs over, the one named last changes fastest.
Arguments:
- integrals: bfloat16 [8, 32, 60, 128, 128], P(None, 'row', 'rep', 'col'), may hold values from -0.0625 to 0.0625
- amplitudes: bfloat16 [8, 16, 60, 128, 128], P(None, 'col', 'rep', 'row'), may hold values from -6 to 6
- virt_count: int32 [8], replicated, may hold values from 76 to 128, as said below
- occ_irrep: int32 [60], replicated, may hold values from 0 to 7
Outputs:
- cycle: bfloat16 [8, 32, 128, 16, 128], P('rep', 'row', None, 'col')
Inputs may be any that keep to these rules, and one draw needn't show every extreme that they name: `virt_count`: one irrep has exactly 128 virtual orbitals.
All inputs are finite; a program needn't handle non-finite values.
Results may differ from a plain program's by a relative error of at most 0.001.
Values may be sent and summed in bfloat16 or wider, within the bound.
No kernel may reach another device: no remote copies, remote signals or barrier semaphores. Data moves between devices by JAX's collectives and lax.ppermute only.
A program may use at most 128 MiB of HBM per device.

v0:
```python
import jax
import jax.numpy as jnp
from jax import lax
from jax.sharding import PartitionSpec as P


def contract(w_part, t_part):
    w_full = lax.all_gather(w_part, "col", axis=3, tiled=True)
    return jnp.einsum(
        "gikca,gjkcb->giajb",
        w_full,
        lax.all_gather(t_part, "row", axis=3, tiled=True),
        preferred_element_type=jnp.float32,
    )


def body(integrals, amplitudes, virt_count, occ_irrep):
    ngroup = integrals.shape[0]
    k_local = integrals.shape[2]
    c_local = integrals.shape[3]
    nvirt = integrals.shape[4]
    rep_index = lax.axis_index("rep")
    col_index = lax.axis_index("col")
    occ_local = lax.dynamic_slice_in_dim(occ_irrep, rep_index * k_local, k_local)
    groups = jnp.arange(ngroup, dtype=jnp.int32)
    blocks = jnp.bitwise_xor(groups[:, None], occ_local[None, :])
    onehot = blocks[:, :, None] == groups[None, None, :]
    limit = jnp.sum(jnp.where(onehot, virt_count[None, None, :], 0), axis=2)
    c_global = col_index * c_local + jnp.arange(c_local, dtype=jnp.int32)
    c_live = c_global[None, None, :] < limit[:, :, None]
    places = jnp.arange(nvirt, dtype=jnp.int32)
    a_live = places[None, :] < virt_count[:, None]
    keep = c_live[:, None, :, :, None] & a_live[:, None, None, None, :]
    masked = jnp.where(keep, integrals, jnp.zeros_like(integrals))
    owned = ngroup // lax.axis_size("rep")
    partial_cycle = contract(masked, amplitudes)
    summed = lax.psum_scatter(partial_cycle, "rep", scatter_dimension=0, tiled=True)
    own_counts = lax.dynamic_slice_in_dim(virt_count, rep_index * owned, owned)
    b_live = places[None, :] < own_counts[:, None]
    result = jnp.where(b_live[:, None, None, None, :], summed, jnp.zeros_like(summed))
    return result.astype(jnp.bfloat16)


def solution(mesh):
    return jax.shard_map(
        body,
        mesh=mesh,
        in_specs=(P(None, "row", "rep", "col", None), P(None, "col", "rep", "row", None), P(), P()),
        out_specs=P("rep", "row", None, "col", None),
        check_vma=False,
    )
```

profile of v0, /device:TPU:1, one launch (start us, length us, event | category | flops | bytes accessed | tf_op | source)
XLA Modules:
  0.0 377.3 jit_solution(17503319874373990578)
XLA Ops:
  6.5 0.0 all-gather.3.cloned.1.call-start
  6.5 0.7 iota_compare_fusion.1
  7.3 0.7 dynamic_slice.7
  8.0 0.7 select_reduce_fusion
  8.7 0.1 broadcast_compare_fusion
  8.8 0.8 broadcast_and_fusion
  9.6 3.1 broadcast_select_fusion
  12.7 0.0 all-gather.3.cloned.1.call-update
  12.8 0.0 all-gather.5.cloned.1.call-start
  12.8 0.7 all-gather.5.cloned.1.call-update
  13.5 0.0 copy-start
  13.5 0.0 reduce-scatter.2.cloned.1.call-start
  13.6 84.3 %all-gather.3.cloned.1.call-done = bf16[8,2,15,128,128]{4,3,2,1,0:T(8,128)(2,1)} async-done(((bf16[8,2,15,32,128]{4,3,2,1,0:T(8,128)(2,1)}), bf16[8,2,15,128,128]{4,3,2,1,0:T(8,128)(2,1)}) %all-gather.3.cloned.1.call-update) | async-done | bytes 7864336 | tf_op jit(solution)/shard_map/all_gather | solution.py:8
  97.8 179.9 %all-gather.5.cloned.1.call-done = bf16[8,4,15,128,128]{4,3,2,1,0:T(8,128)(2,1)} async-done(((bf16[8,4,15,8,128]{4,3,2,1,0:T(8,128)(2,1)}), bf16[8,4,15,128,128]{4,3,2,1,0:T(8,128)(2,1)}) %all-gather.5.cloned.1.call-update) | async-done | bytes 15728656 | tf_op jit(solution)/shard_map/all_gather | solution.py:12
  277.7 14.3 %fusion.3 = f32[8,2,128,4,128]{4,2,3,1,0:T(8,128)} fusion(bf16[8,4,15,128,128]{4,3,2,1,0:T(8,128)(2,1)} %all-gather.5.cloned.1.call-done, bf16[8,2,15,128,128]{4,3,2,1,0:T(8,128)(2,1)} %all-gather.3.cloned.1.call-done), kind=kOutput, calls=%fused_computation.3 | convolution fusion | flops 4026531840 | bytes 27787264 | tf_op jit(solution)/shard_map/gikca,gjkcb->giajb/dot_general | solution.py:9
  292.0 0.0 reduce-scatter.2.cloned.1.call-update
  292.1 0.0 copy-done
  292.1 0.1 dynamic_slice.6
  292.2 0.1 iota_compare_fusion.2
  292.2 76.0 %reduce-scatter.2.cloned.1.call-done = f32[2,2,128,4,128]{4,2,3,1,0:T(8,128)} async-done(((f32[8,2,128,4,128]{4,2,3,1,0:T(8,128)}), f32[2,2,128,4,128]{4,2,3,1,0:T(8,128)}) %reduce-scatter.2.cloned.1.call-update) | async-done | bytes 1048592 | tf_op jit(solution)/shard_map/reduce_scatter | solution.py:37
  368.2 1.3 select_convert_fusion
  369.6 1.2 copy.6
  (2 shorter events, 0.0 us)
Async XLA Ops:
  6.5 91.3 %all-gather.3.cloned.1.call-start = ((), (), s32[]{:S(2)}) async-start(), calls=%async_computation.1 | async-start | bytes 9830400 | tf_op jit(solution)/shard_map/all_gather | solution.py:8
  12.8 265.0 %all-gather.5.cloned.1.call-start = ((), (), s32[]{:S(2)}) async-start(), calls=%async_computation.2 | async-start | bytes 16711680 | tf_op jit(solution)/shard_map/all_gather | solution.py:12
  13.5 278.6 %copy-start = (s32[8]{0:T(128)S(1)}, s32[8]{0:T(128)}, u32[]{:S(2)}) copy-start(s32[8]{0:T(128)} %param.6) | copy-start | bytes 100
  13.5 354.7 %reduce-scatter.2.cloned.1.call-start = ((), (), s32[]{:S(2)}) async-start(), calls=%async_computation.3 | async-start | bytes 5242880 | tf_op jit(solution)/shard_map/reduce_scatter | solution.py:37
Sparse Core Ops, SparseCore 0:
  12.9 84.8 all-gather.2
  100.4 177.3 all-gather.4
  292.2 75.9 reduce-scatter.1
where the time goes:
time: 377 us
  waiting for transfers between devices  341 us (90%)
  matrix products  14.3 us (4%)
  between operations  13.2 us (4%)
  other arithmetic  6.86 us (2%)
    all_gather x1, waiting for transfers between devices, contract(): lax.all_gather(t_part, 'row', axis=3, tiled=True)  180 us
    all_gather x1, waiting for transfers between devices, contract(): w_full = lax.all_gather(w_part, 'col', axis=3, tiled=True)  84.3 us
    reduce_scatter x1, waiting for transfers between devices, body(): lax.psum_scatter(partial_cycle, 'rep', scatter_dimension=0, tiled=True)  76 us
    dot_general x1, matrix products, contract(): jnp.einsum('gikca,gjkcb->giajb', w_full, lax.all_gather(t_part, 'row', ax...  14.3 us
  transfers between devices with their start and end apart: 3, of which 3 were waited for; matrix products, arithmetic and copies ran while one was open for 0% of the time, Pallas kernels for 0%

commit v1 on v0

--- a/solution.py
+++ b/solution.py
@@ -5,7 +5,9 @@
 
 
 def contract(w_part, t_part):
-    w_full = lax.all_gather(w_part, "col", axis=3, tiled=True)
+    w_full = jnp.concatenate(
+        jax.lax.all_to_all(jnp.stack(jax.lax.axis_size("col") * [w_part]), "col", 0, 0), axis=3
+    )
     return jnp.einsum(
         "gikca,gjkcb->giajb",
         w_full,

time: 377 us -> 290 us (0.77)
  waiting for transfers between devices: 341 us -> 155 us
  blocking collectives: 0 us -> 92 us
  local copies, waits for them, and re-layouts: 2.01 us -> 9.45 us
    all_gather x1, waiting for transfers between devices: 180 us -> 78.4 us  [contract(): lax.all_gather(t_part, 'row', axis=3, tiled=True)]
    all_to_all x0 -> x1, blocking collectives: none -> 92 us  [contract(): jax.lax.all_to_all(jnp.stack(jax.lax.axis_size('col') * [w_part]), 'col',...]
    all_gather x1 -> x0, waiting for transfers between devices: 84.3 us -> none  [contract(): w_full = lax.all_gather(w_part, 'col', axis=3, tiled=True)]
    all_to_all x0 -> x1, local copies, waits for them, and re-layouts: none -> 5.32 us  [contract(): jax.lax.all_to_all(jnp.stack(jax.lax.axis_size('col') * [w_part]), 'col',...]
  transfers between devices with their start and end apart: 3 -> 2, of which waited for: 3 -> 2; matrix products, arithmetic and copies ran while one was open for 0% -> 4% of each run, Pallas kernels for 0% -> 0%
where the time goes in v1:
time: 290 us
  waiting for transfers between devices  155 us (53%)
  blocking collectives  92 us (32%)
  matrix products  14.3 us (5%)
  between operations  13.5 us (5%)
  local copies, waits for them, and re-layouts  9.45 us (3%)
  other arithmetic  5.49 us (2%)
    all_to_all x1, blocking collectives, contract(): jax.lax.all_to_all(jnp.stack(jax.lax.axis_size('col') * [w_part]), 'col',...  92 us
    all_gather x1, waiting for transfers between devices, contract(): lax.all_gather(t_part, 'row', axis=3, tiled=True)  78.4 us
    reduce_scatter x1, waiting for transfers between devices, body(): lax.psum_scatter(partial_cycle, 'rep', scatter_dimension=0, tiled=True)  76 us
    dot_general x1, matrix products, contract(): jnp.einsum('gikca,gjkcb->giajb', w_full, lax.all_gather(t_part, 'row', ax...  14.3 us
  transfers between devices with their start and end apart: 2, of which 2 were waited for; matrix products, arithmetic and copies ran while one was open for 4% of the time, Pallas kernels for 0%

profile of v1, /device:TPU:1, one launch (start us, length us, event | category | flops | bytes accessed | tf_op | source)
XLA Modules:
  0.0 289.9 jit_solution(8959882487910101929)
XLA Ops:
  6.5 0.0 all-gather.2.cloned.1.call-start
  6.5 0.7 all-gather.2.cloned.1.call-update
  7.3 0.0 reduce-scatter.2.cloned.1.call-start
  7.3 0.7 dynamic_slice.7
  8.0 0.7 select_reduce_fusion
  8.8 0.7 iota_compare_fusion.1
  9.5 0.1 broadcast_compare_fusion
  9.6 0.8 broadcast_and_fusion
  10.4 1.7 broadcast_select_fusion
  12.1 2.1 stack.2
  14.3 92.0 %all_to_all.5 = bf16[4,8,2,15,32,128]{5,4,3,2,1,0:T(8,128)(2,1)S(1)} all-to-all(bf16[4,8,2,15,32,128]{5,4,3,2,1,0:T(8,128)(2,1)S(1)} %stack.2), channel_id=1, replica_groups=mesh['row'=16,'col'=4,'rep'=4] {'col'}, dimensions={0} | all-to-all | bytes 15728640 | tf_op jit(solution)/shard_map/all_to_all | solution.py:9
  106.3 5.3 %copy.12 = bf16[4,8,2,15,32,128]{5,4,0,3,2,1:T(8,128)(2,1)} copy(bf16[4,8,2,15,32,128]{5,4,3,2,1,0:T(8,128)(2,1)S(1)} %all_to_all.5) | data formatting | bytes 15728640 | tf_op jit(solution)/shard_map/all_to_all | solution.py:9
  111.6 78.4 %all-gather.2.cloned.1.call-done = bf16[8,4,15,128,128]{4,3,2,1,0:T(8,128)(2,1)} async-done(((bf16[8,4,15,8,128]{4,3,2,1,0:T(8,128)(2,1)}), bf16[8,4,15,128,128]{4,3,2,1,0:T(8,128)(2,1)}) %all-gather.2.cloned.1.call-update) | async-done | bytes 15728656 | tf_op jit(solution)/shard_map/all_gather | solution.py:14
  190.0 0.0 copy-start
  190.0 14.3 %fusion.2 = f32[8,2,128,4,128]{4,2,3,1,0:T(8,128)} fusion(bf16[8,2,15,128,128,1]{4,3,2,5,1,0:T(8,128)(2,1)} %bitcast.18, bf16[8,4,15,128,128]{4,3,2,1,0:T(8,128)(2,1)} %all-gather.2.cloned.1.call-done), kind=kOutput, calls=%fused_computation.2 | convolution fusion | flops 4026531840 | bytes 27787264 | tf_op jit(solution)/shard_map/gikca,gjkcb->giajb/dot_general | solution.py:11
  204.3 0.0 reduce-scatter.2.cloned.1.call-update
  204.3 0.0 copy-done
  204.3 0.1 dynamic_slice.6
  204.4 0.1 iota_compare_fusion.2
  204.5 76.0 %reduce-scatter.2.cloned.1.call-done = f32[2,2,128,4,128]{4,2,3,1,0:T(8,128)} async-done(((f32[8,2,128,4,128]{4,2,3,1,0:T(8,128)}), f32[2,2,128,4,128]{4,2,3,1,0:T(8,128)}) %reduce-scatter.2.cloned.1.call-update) | async-done | bytes 1048592 | tf_op jit(solution)/shard_map/reduce_scatter | solution.py:39
  280.5 1.3 select_convert_fusion
  281.8 1.2 copy.14
  (2 shorter events, 0.0 us)
Async XLA Ops:
  6.5 183.4 %all-gather.2.cloned.1.call-start = ((), (), s32[]{:S(2)}) async-start(), calls=%async_computation.2 | async-start | bytes 16711680 | tf_op jit(solution)/shard_map/all_gather | solution.py:14
  7.3 273.2 %reduce-scatter.2.cloned.1.call-start = ((), (), s32[]{:S(2)}) async-start(), calls=%async_computation.3 | async-start | bytes 5242880 | tf_op jit(solution)/shard_map/reduce_scatter | solution.py:39
  190.0 14.3 %copy-start = (s32[8]{0:T(128)S(1)}, s32[8]{0:T(128)}, u32[]{:S(2)}) copy-start(s32[8]{0:T(128)} %param.6) | copy-start | bytes 100
Sparse Core Ops, SparseCore 0:
  9.9 180.0 all-gather.1
  204.4 76.0 reduce-scatter.1
